TPU v7x, 128 devices: a whole 4x4x4 slice. The times are simulated.
128 devices in a mesh: ma: 16 (over x, z), band: 8 (over y, core).
Axes of the slice: x: 4, y: 4, z: 4, core: 2. Of those that a mesh axis runs over, the one named last changes fastest.
Arguments:
- harmonics: bfloat16 [128, 8192, 256], P(('ma', 'band')), may hold values from -6 to 6
- legendre: bfloat16 [128, 2, 8192, 512], P(('ma', 'band')), may hold values from -0.0029296875 to 0.0029296875
- m_values: int32 [128], replicated, may hold values from 1 to 8191
- cycle_cell: int32 [16384], P(('ma', 'band')), may hold values from 0 to 63, as said below
- phi_cell: int32 [16384], P(('ma', 'band')), may hold values from 3 to 123
- offsets: float32 [2, 16384], P(None, ('ma', 'band')), may hold values from 0 to 1
Outputs:
- lensed: float32 [16384, 128], P(('ma', 'band'))
Inputs may be any that keep to these rules, and one draw needn't show every extreme that they name: `cycle_cell`: Band-local cycle; every point held by device (ma, band) lies in latitude band `band`. For each device and each ma index q, at most 16 of its points have cycles q * 4 to q * 4 + 3, and in every band one q receives exactly 16 points from every device of the band.
All inputs are finite; a program needn't handle non-finite values.
Results may differ from a plain program's by a relative error of at most 0.0053.
Values may be sent and summed in bfloat16 or wider, within the bound.
No kernel may reach another device: no remote copies, remote signals or barrier semaphores. Data moves between devices by JAX's collectives and lax.ppermute only.
A program may use at most 64 MiB of HBM per device.

v0:
```python
import jax
import jax.numpy as jnp
from jax import lax
from jax.sharding import PartitionSpec as P

NPHI = 128


def with_halo(x, sides, width):
    for axis, dim in sides:
        count, length = (lax.axis_size(axis), x.shape[dim])
        up = [(i, (i + 1) % count) for i in range(count - 1)]
        down = [(j, i) for i, j in up]
        last = lax.slice_in_dim(x, length - width, length, axis=dim)
        first = lax.slice_in_dim(x, 0, width, axis=dim)
        before = lax.ppermute(last, axis, up)
        after = lax.ppermute(first, axis, down)
        x = jnp.concatenate([before, x, after], axis=dim)
    return x


def kernel_taps(shifts):
    return jnp.sinc(shifts) * jnp.sinc(shifts / 4.0)


def combine_parts(plus_part, minus_part):
    q_real = -(plus_part[:, 0, 0] - minus_part[:, 1, 1])
    q_imag = -(plus_part[:, 0, 1] + minus_part[:, 1, 0])
    u_real = -(plus_part[:, 1, 0] + minus_part[:, 0, 1])
    u_imag = -(plus_part[:, 1, 1] - minus_part[:, 0, 0])
    real_part = jnp.concatenate([q_real, u_real], axis=1)
    imag_part = jnp.concatenate([q_imag, u_imag], axis=1)
    return jnp.stack([real_part, imag_part], axis=1).astype(jnp.bfloat16)


def phase_table(m_values, cell_count, lmax_width):
    pixel_index = jnp.arange(cell_count, dtype=jnp.int32)
    period = 2 * lmax_width
    phase_turns = m_values[None, :] * pixel_index[:, None] % period
    angles = phase_turns.astype(jnp.float32) * (2.0 * jnp.pi / period)
    return jnp.stack([jnp.cos(angles), -jnp.sin(angles)], axis=-1).astype(jnp.bfloat16)


def spectral_cycles(phase_rows, spectra):
    summed = jnp.einsum("kmi,mric->rkc", phase_rows, spectra, preferred_element_type=jnp.float32)
    return (2.0 * summed).astype(jnp.bfloat16)


def spread_weights(starts, weights, length):
    tap_index = jnp.arange(8, dtype=jnp.int32)
    target = starts[:, None] + tap_index[None, :]
    cells = jnp.arange(length, dtype=jnp.int32)
    hits = (target[:, :, None] == cells[None, None, :]).astype(jnp.float32)
    return jnp.sum(weights[:, :, None] * hits, axis=1)


def on_device(harmonics, legendre, m_values, cycle_cell, phi_cell, offsets):
    evolutions = harmonics.shape[2] // 4
    cycle_total = legendre.shape[3]
    contract = (((0,), (0,)), ((), ()))
    plus_part = lax.dot_general(
        legendre[0, 0], harmonics[0], contract, preferred_element_type=jnp.float32
    )
    minus_part = lax.dot_general(
        legendre[0, 1], harmonics[0], contract, preferred_element_type=jnp.float32
    )
    spectra = combine_parts(
        plus_part.reshape(cycle_total, 2, 2, evolutions),
        minus_part.reshape(cycle_total, 2, 2, evolutions),
    )
    width_out = spectra.shape[2]
    owner_count = lax.axis_size("ma")
    band_count = lax.axis_size("band")
    cycle_depth = cycle_total // (owner_count * band_count)
    received = lax.all_to_all(
        spectra[None], ("ma", "band"), split_axis=1, concat_axis=0, tiled=True
    )
    phase_rows = phase_table(m_values, NPHI, harmonics.shape[1])
    own_grid = spectral_cycles(phase_rows, received)
    extended = with_halo(own_grid, (("ma", 0),), 4)
    ext_rows = extended.shape[0]
    flat_grid = extended.reshape(ext_rows * NPHI, width_out)
    first_cycle = lax.axis_index("ma") * cycle_depth
    capacity = cycle_cell.shape[0] // 8
    owner_index = cycle_cell // cycle_depth
    one_hot = (owner_index[:, None] == jnp.arange(owner_count, dtype=jnp.int32)[None, :]).astype(
        jnp.int32
    )
    slot_index = jnp.sum((jnp.cumsum(one_hot, axis=0) - one_hot) * one_hot, axis=1)
    flat_slot = owner_index * capacity + slot_index
    placement = (
        flat_slot[:, None] == jnp.arange(owner_count * capacity, dtype=jnp.int32)[None, :]
    ).astype(jnp.float32)
    point_table = jnp.stack(
        [cycle_cell.astype(jnp.float32), phi_cell.astype(jnp.float32), offsets[0], offsets[1]],
        axis=1,
    )
    buffers = jnp.dot(placement.T, point_table, precision=lax.Precision.HIGHEST).reshape(
        owner_count, capacity, 4
    )
    cycle_buffer = buffers[:, :, 0].astype(jnp.int32)
    phi_buffer = buffers[:, :, 1].astype(jnp.int32)
    offset_buffer = buffers[:, :, 2:4]
    cycles_here = lax.all_to_all(cycle_buffer, "ma", split_axis=0, concat_axis=0, tiled=True)
    phis_here = lax.all_to_all(phi_buffer, "ma", split_axis=0, concat_axis=0, tiled=True)
    offsets_here = lax.all_to_all(offset_buffer, "ma", split_axis=0, concat_axis=0, tiled=True)
    sources, items = cycles_here.shape
    cycles_flat = cycles_here.reshape(-1)
    phis_flat = phis_here.reshape(-1)
    pairs = offsets_here.reshape(-1, 2)
    tap_shift = jnp.arange(8).astype(jnp.float32) - 3.0
    across = kernel_taps(tap_shift[None, :] - pairs[:, 0:1])
    beside_all = kernel_taps(tap_shift[None, :] - pairs[:, 1:2])
    cycle_weights = spread_weights(cycles_flat + 1 - first_cycle, across, ext_rows)
    phi_weights = spread_weights(phis_flat - 3, beside_all, NPHI)
    dense = (cycle_weights[:, :, None] * phi_weights[:, None, :]).astype(jnp.bfloat16)
    dense = dense.reshape(cycles_flat.shape[0], ext_rows * NPHI)
    values = jnp.dot(dense, flat_grid, preferred_element_type=jnp.float32)
    values = values.reshape(sources, items, width_out)
    returned = lax.all_to_all(values, "ma", split_axis=0, concat_axis=0, tiled=True)
    return jnp.dot(
        placement,
        returned.reshape(owner_count * capacity, width_out),
        precision=lax.Precision.HIGHEST,
    )


def solution(mesh):
    in_specs = (
        P(("ma", "band"), None, None),
        P(("ma", "band"), None, None, None),
        P(),
        P(("ma", "band")),
        P(("ma", "band")),
        P(None, ("ma", "band")),
    )
    out_specs = P(("ma", "band"), None)
    return jax.shard_map(
        on_device, mesh=mesh, in_specs=in_specs, out_specs=out_specs, check_vma=False
    )
```

profile of v0, /device:TPU:0, one launch (start us, length us, event | category | flops | bytes accessed | tf_op | source)
XLA Modules:
  0.0 100.5 jit_solution(4948932564756850836)
XLA Ops:
  0.0 0.7 convert_bitcast_fusion.1
  0.7 0.1 fusion.33
  0.8 0.2 reduce_window_sum.11
  1.0 0.2 select_reduce_fusion.2
  1.2 0.8 slice_bitcast_fusion.1
  2.0 0.7 convert_bitcast_fusion
  2.6 0.2 fusion.19
  2.8 0.1 reshape.275
  2.9 0.6 slice_convert_fusion.1
  3.5 8.0 %all-to-all-start = ((s32[16,1,16]{2,1,0:T(1,128)}), s32[16,1,16]{2,1,0:T(1,128)S(1)}, u32[]{:S(2)}, u32[]{:S(2)}) async-start(s32[16,1,16]{2,1,0:T(1,128)} %bitcast.4), calls=%async_computation | async-start | bytes 16384 | tf_op jit(solution)/shard_map/all_to_all | solution.py:104
  11.5 6.4 %copy.40 = bf16[1,8192,256]{1,2,0:T(8,128)(2,1)} copy(bf16[1,8192,256]{2,1,0:T(8,128)(2,1)} %param.7) | data formatting | bytes 8388608 | tf_op args[0]
  17.9 0.0 copy-start
  17.9 0.0 copy-start.2
  17.9 7.0 %fusion = f32[512,2,2,64]{0,3,2,1:T(8,128)S(1)} fusion(bf16[2,2,64,8192]{3,2,1,0:T(8,128)(2,1)} %bitcast.73, bf16[1,2,8192,512]{3,2,1,0:T(8,128)(2,1)} %param.8), kind=kOutput, calls=%fused_computation | convolution fusion | flops 2147483648 | bytes 13107200 | tf_op jit(solution)/shard_map/dot_general | solution.py:64
  25.0 0.0 copy-done
  25.0 3.6 %copy-done.2 = bf16[1,2,8192,512]{3,2,1,0:T(8,128)(2,1)S(1)} copy-done((bf16[1,2,8192,512]{3,2,1,0:T(8,128)(2,1)S(1)}, bf16[1,2,8192,512]{3,2,1,0:T(8,128)(2,1)}, u32[]{:S(2)}) %copy-start.2) | copy-done | bytes 16777240
  28.5 2.3 %fusion.2 = f32[512,2,2,64]{0,3,2,1:T(8,128)S(1)} fusion(bf16[2,2,64,8192]{3,2,1,0:T(8,128)(2,1)S(1)} %bitcast.74, bf16[1,2,8192,512]{3,2,1,0:T(8,128)(2,1)S(1)} %copy-done.2), kind=kOutput, calls=%fused_computation.2 | convolution fusion | flops 2147483648 | bytes 13107200 | tf_op jit(solution)/shard_map/dot_general | solution.py:61
  30.9 0.0 copy-done.1
  30.9 0.3 cosine_convert_fusion
  31.2 0.1 fusion.23
  31.3 0.0 all-to-all-done
  31.4 7.2 %all-to-all-start.2 = ((s32[16,1,16]{2,1,0:T(1,128)}), s32[16,1,16]{2,1,0:T(1,128)S(1)}, u32[]{:S(2)}, u32[]{:S(2)}) async-start(s32[16,1,16]{2,1,0:T(1,128)} %bitcast.7), calls=%async_computation.2 | async-start | bytes 16384 | tf_op jit(solution)/shard_map/all_to_all | solution.py:105
  38.6 0.9 copy.41
  39.5 0.6 copy.35
  40.1 6.1 %all-to-all-done.2 = s32[16,1,16]{2,1,0:T(1,128)S(1)} async-done(((s32[16,1,16]{2,1,0:T(1,128)}), s32[16,1,16]{2,1,0:T(1,128)S(1)}, u32[]{:S(2)}, u32[]{:S(2)}) %all-to-all-start.2) | async-done | bytes 1056 | tf_op jit(solution)/shard_map/all_to_all | solution.py:105
  46.2 3.5 %all-to-all-start.1 = ((f32[16,16,2]{1,2,0:T(2,128)}), f32[16,16,2]{1,2,0:T(2,128)S(1)}, u32[]{:S(2)}, u32[]{:S(2)}) async-start(f32[16,16,2]{1,2,0:T(2,128)} %copy.35), calls=%async_computation.1 | async-start | bytes 32768 | tf_op jit(solution)/shard_map/all_to_all | solution.py:106
  49.7 0.1 add_reduce_fusion
  49.7 0.1 sub.81
  49.8 0.1 sub.88
  49.9 0.1 iota_add_fusion
  50.0 7.2 %all-to-all-done.1 = f32[16,16,2]{1,2,0:T(2,128)S(1)} async-done(((f32[16,16,2]{1,2,0:T(2,128)}), f32[16,16,2]{1,2,0:T(2,128)S(1)}, u32[]{:S(2)}, u32[]{:S(2)}) %all-to-all-start.1) | async-done | bytes 2080 | tf_op jit(solution)/shard_map/all_to_all | solution.py:106
  57.2 6.4 %all-to-all-start.3 = ((bf16[1,512,2,128]{3,2,0,1:T(2,128)(2,1)}), bf16[1,512,2,128]{3,2,0,1:T(2,128)(2,1)S(1)}, u32[]{:S(2)}, u32[]{:S(2)}) async-start(bf16[1,512,2,128]{3,2,0,1:T(2,128)(2,1)} %copy.41), calls=%async_computation.3 | async-start | bytes 524288 | tf_op jit(solution)/shard_map/all_to_all | solution.py:75
  63.7 0.1 reshape.276
  63.8 0.1 fusion.59
  63.9 0.1 copy.37
  64.0 0.1 copy.39
  64.2 1.3 %select_reduce_fusion = f32[256,128]{1,0:T(8,128)S(1)} fusion(f32[256,8]{1,0:T(8,128)S(1)} %copy.39, s32[256,8]{1,0:T(8,128)S(1)} %iota_add_fusion), kind=kLoop, calls=%fused_computation.11 | loop fusion | flops 753664 | bytes 147456 | tf_op jit(solution)/shard_map/reduce_sum | solution.py:54
  65.4 8.9 %all-to-all-done.3 = bf16[1,512,2,128]{3,2,0,1:T(2,128)(2,1)S(1)} async-done(((bf16[1,512,2,128]{3,2,0,1:T(2,128)(2,1)}), bf16[1,512,2,128]{3,2,0,1:T(2,128)(2,1)S(1)}, u32[]{:S(2)}, u32[]{:S(2)}) %all-to-all-start.3) | async-done | bytes 262176 | tf_op jit(solution)/shard_map/all_to_all | solution.py:75
  74.4 0.2 fusion.8
  74.6 2.7 %collective-permute-start = (bf16[4,128,128]{2,1,0:T(8,128)(2,1)S(1)}, bf16[4,128,128]{2,1,0:T(8,128)(2,1)S(1)}, u32[]{:S(2)}, u32[]{:S(2)}) collective-permute-start(bf16[4,128,128]{2,1,0:T(8,128)(2,1)S(1)} %fusion.8), channel_id=1, source_target_pairs={{0,8},{8,16},{16,24},{24,32},{32,40},{40,48},{48,56},{56,64},{64,7... | collective-permute-start | bytes 393224 | tf_op jit(solution)/shard_map/ppermute | solution.py:16
  77.3 1.3 %collective-permute-start.1 = (bf16[4,128,128]{2,1,0:T(8,128)(2,1)S(1)}, bf16[4,128,128]{2,1,0:T(8,128)(2,1)S(1)}, u32[]{:S(2)}, u32[]{:S(2)}) collective-permute-start(bf16[4,128,128]{2,1,0:T(8,128)(2,1)S(1)} %fusion.8), channel_id=1, source_target_pairs={{8,0},{16,8},{24,16},{32,24},{40,32},{48,40},{56,48},{64,56},{72,6... | collective-permute-start | bytes 393224 | tf_op jit(solution)/shard_map/ppermute | solution.py:17
  78.6 0.7 multiply_convert_fusion
  79.3 0.5 convert_element_type.102
  79.9 0.0 collective-permute-done
  79.9 4.3 %collective-permute-done.1 = bf16[4,128,128]{2,1,0:T(8,128)(2,1)S(1)} collective-permute-done((bf16[4,128,128]{2,1,0:T(8,128)(2,1)S(1)}, bf16[4,128,128]{2,1,0:T(8,128)(2,1)S(1)}, u32[]{:S(2)}, u32[]{:S(2)}) %collective-permute-start.1) | collective-permute-done | bytes 131104 | tf_op jit(solution)/shard_map/ppermute | solution.py:17
  84.2 0.4 fusion.131
  84.6 15.0 %all_to_all.34 = f32[16,16,128]{2,1,0:T(8,128)S(1)} all-to-all(f32[16,16,128]{2,1,0:T(8,128)S(1)} %fusion.131), channel_id=1, replica_groups=mesh['ma'=16,'band'=8] {'ma'}, dimensions={0} | all-to-all | bytes 262144 | tf_op jit(solution)/shard_map/all_to_all | solution.py:120
  99.6 0.9 fusion.18
  (11 shorter events, 0.2 us)
Async XLA Ops:
  3.5 27.8 %all-to-all-start = ((s32[16,1,16]{2,1,0:T(1,128)}), s32[16,1,16]{2,1,0:T(1,128)S(1)}, u32[]{:S(2)}, u32[]{:S(2)}) async-start(s32[16,1,16]{2,1,0:T(1,128)} %bitcast.4), calls=%async_computation | async-start | bytes 16384 | tf_op jit(solution)/shard_map/all_to_all | solution.py:104
  17.9 7.1 %copy-start = (bf16[1,8192,256]{1,2,0:T(8,128)(2,1)S(1)}, bf16[1,8192,256]{1,2,0:T(8,128)(2,1)}, u32[]{:S(2)}) copy-start(bf16[1,8192,256]{1,2,0:T(8,128)(2,1)} %copy.40) | copy-start | bytes 12582916
  17.9 10.6 %copy-start.2 = (bf16[1,2,8192,512]{3,2,1,0:T(8,128)(2,1)S(1)}, bf16[1,2,8192,512]{3,2,1,0:T(8,128)(2,1)}, u32[]{:S(2)}) copy-start(bf16[1,2,8192,512]{3,2,1,0:T(8,128)(2,1)} %param.8) | copy-start | bytes 50331652
  28.5 2.3 %copy-start.1 = (s32[128]{0:T(128)S(1)}, s32[128]{0:T(128)}, u32[]{:S(2)}) copy-start(s32[128]{0:T(128)} %param.9) | copy-start | bytes 1540
  31.4 14.8 %all-to-all-start.2 = ((s32[16,1,16]{2,1,0:T(1,128)}), s32[16,1,16]{2,1,0:T(1,128)S(1)}, u32[]{:S(2)}, u32[]{:S(2)}) async-start(s32[16,1,16]{2,1,0:T(1,128)} %bitcast.7), calls=%async_computation.2 | async-start | bytes 16384 | tf_op jit(solution)/shard_map/all_to_all | solution.py:105
  46.2 11.0 %all-to-all-start.1 = ((f32[16,16,2]{1,2,0:T(2,128)}), f32[16,16,2]{1,2,0:T(2,128)S(1)}, u32[]{:S(2)}, u32[]{:S(2)}) async-start(f32[16,16,2]{1,2,0:T(2,128)} %copy.35), calls=%async_computation.1 | async-start | bytes 32768 | tf_op jit(solution)/shard_map/all_to_all | solution.py:106
  57.2 17.2 %all-to-all-start.3 = ((bf16[1,512,2,128]{3,2,0,1:T(2,128)(2,1)}), bf16[1,512,2,128]{3,2,0,1:T(2,128)(2,1)S(1)}, u32[]{:S(2)}, u32[]{:S(2)}) async-start(bf16[1,512,2,128]{3,2,0,1:T(2,128)(2,1)} %copy.41), calls=%async_computation.3 | async-start | bytes 524288 | tf_op jit(solution)/shard_map/all_to_all | solution.py:75
  74.6 5.3 %collective-permute-start = (bf16[4,128,128]{2,1,0:T(8,128)(2,1)S(1)}, bf16[4,128,128]{2,1,0:T(8,128)(2,1)S(1)}, u32[]{:S(2)}, u32[]{:S(2)}) collective-permute-start(bf16[4,128,128]{2,1,0:T(8,128)(2,1)S(1)} %fusion.8), channel_id=1, source_target_pairs={{0,8},{8,16},{16,24},{24,32},{32,40},{40,48},{48,56},{56,64},{64,7... | collective-permute-start | bytes 393224 | tf_op jit(solution)/shard_map/ppermute | solution.py:16
  77.3 6.9 %collective-permute-start.1 = (bf16[4,128,128]{2,1,0:T(8,128)(2,1)S(1)}, bf16[4,128,128]{2,1,0:T(8,128)(2,1)S(1)}, u32[]{:S(2)}, u32[]{:S(2)}) collective-permute-start(bf16[4,128,128]{2,1,0:T(8,128)(2,1)S(1)} %fusion.8), channel_id=1, source_target_pairs={{8,0},{16,8},{24,16},{32,24},{40,32},{48,40},{56,48},{64,56},{72,6... | collective-permute-start | bytes 393224 | tf_op jit(solution)/shard_map/ppermute | solution.py:17
where the time goes:
time: 101 us
  starting transfers between devices  29.2 us (29%)
  waiting for transfers between devices  26.5 us (26%)
  blocking collectives  15 us (15%)
  local copies, waits for them, and re-layouts  13.3 us (13%)
  matrix products  11 us (11%)
  other arithmetic  5.22 us (5%)
    all_to_all x1, blocking collectives, on_device(): lax.all_to_all(values, 'ma', split_axis=0, concat_axis=0, tiled=True)  15 us
    unnamed x7, local copies, waits for them, and re-layouts  9.96 us
    all_to_all x1, waiting for transfers between devices, on_device(): lax.all_to_all(spectra[None], ('ma', 'band'), split_axis=1, concat_axis=0...  8.95 us
    all_to_all x1, starting transfers between devices, on_device(): lax.all_to_all(cycle_buffer, 'ma', split_axis=0, concat_axis=0, tiled=True)  7.99 us
    all_to_all x1, starting transfers between devices, on_device(): lax.all_to_all(phi_buffer, 'ma', split_axis=0, concat_axis=0, tiled=True)  7.22 us
    all_to_all x1, waiting for transfers between devices, on_device(): lax.all_to_all(offset_buffer, 'ma', split_axis=0, concat_axis=0, tiled=True)  7.19 us
    dot_general x1, matrix products, on_device(): lax.dot_general(legendre[0, 1], harmonics[0], contract, preferred_element...  7.04 us
    all_to_all x1, starting transfers between devices, on_device(): lax.all_to_all(spectra[None], ('ma', 'band'), split_axis=1, concat_axis=0...  6.44 us
  transfers between devices with their start and end apart: 6, of which 4 were waited for; matrix products, arithmetic and copies ran while one was open for 21% of the time, Pallas kernels for 0%

commit v1 on v0

--- a/solution.py
+++ b/solution.py
@@ -72,8 +72,14 @@
     owner_count = lax.axis_size("ma")
     band_count = lax.axis_size("band")
     cycle_depth = cycle_total // (owner_count * band_count)
-    received = lax.all_to_all(
-        spectra[None], ("ma", "band"), split_axis=1, concat_axis=0, tiled=True
+    received = jnp.concatenate(
+        lax.all_to_all(
+            jnp.stack(jnp.split(spectra[None], lax.axis_size(("ma", "band")), axis=1)),
+            ("ma", "band"),
+            0,
+            0,
+        ),
+        axis=0,
     )
     phase_rows = phase_table(m_values, NPHI, harmonics.shape[1])
     own_grid = spectral_cycles(phase_rows, received)

time: 101 us -> 195 us (1.93)
  other arithmetic: 5.22 us -> 95.4 us
  local copies, waits for them, and re-layouts: 13.3 us -> 19.5 us
  waiting for transfers between devices: 26.5 us -> 20.5 us
  starting transfers between devices: 29.2 us -> 32.9 us
    unnamed x0 -> x127, other arithmetic: none -> 89.4 us
    another operation x1, local copies, waits for them, and re-layouts: 0.86 us -> 7.01 us  [on_device(): jnp.stack(jnp.split(spectra[None], lax.axis_size(('ma', 'band')), axis=1))]
    all_to_all x1, waiting for transfers between devices: 6.09 us -> 0.01 us  [on_device(): lax.all_to_all(phi_buffer, 'ma', split_axis=0, concat_axis=0, tiled=True)]
    all_to_all x1, starting transfers between devices: 3.5 us -> 7.21 us  [on_device(): lax.all_to_all(offset_buffer, 'ma', split_axis=0, concat_axis=0, tiled=True)]
    unnamed x7 -> x9, local copies, waits for them, and re-layouts: 9.96 us -> 9.98 us
  transfers between devices with their start and end apart: 6 -> 6, of which waited for: 4 -> 3; matrix products, arithmetic and copies ran while one was open for 21% -> 60% of each run, Pallas kernels for 0% -> 0%
where the time goes in v1:
time: 195 us
  other arithmetic  95.4 us (49%)
  starting transfers between devices  32.9 us (17%)
  waiting for transfers between devices  20.5 us (11%)
  local copies, waits for them, and re-layouts  19.5 us (10%)
  blocking collectives  15 us (8%)
  matrix products  11 us (6%)
    unnamed x127, other arithmetic  89.4 us
    all_to_all x1, blocking collectives, on_device(): lax.all_to_all(values, 'ma', split_axis=0, concat_axis=0, tiled=True)  15 us
    unnamed x9, local copies, waits for them, and re-layouts  9.98 us
    all_to_all x1, waiting for transfers between devices, on_device(): lax.all_to_all(jnp.stack(jnp.split(spectra[None], lax.axis_size(('ma', 'b...  8.95 us
    all_to_all x1, starting transfers between devices, on_device(): lax.all_to_all(cycle_buffer, 'ma', split_axis=0, concat_axis=0, tiled=True)  7.99 us
    all_to_all x1, waiting for transfers between devices, on_device(): lax.all_to_all(offset_buffer, 'ma', split_axis=0, concat_axis=0, tiled=True)  7.26 us
    all_to_all x1, starting transfers between devices, on_device(): lax.all_to_all(phi_buffer, 'ma', split_axis=0, concat_axis=0, tiled=True)  7.21 us
    all_to_all x1, starting transfers between devices, on_device(): lax.all_to_all(offset_buffer, 'ma', split_axis=0, concat_axis=0, tiled=True)  7.21 us
  transfers between devices with their start and end apart: 6, of which 3 were waited for; matrix products, arithmetic and copies ran while one was open for 60% of the time, Pallas kernels for 0%

profile of v1, /device:TPU:0, one launch (start us, length us, event | category | flops | bytes accessed | tf_op | source)
XLA Modules:
  0.0 194.5 jit_solution(14473610986437217938)
XLA Ops:
  0.0 0.7 convert_bitcast_fusion.1
  1.2 0.8 slice_bitcast_fusion.1
  3.5 8.0 %all-to-all-start = ((s32[16,1,16]{2,1,0:T(1,128)}), s32[16,1,16]{2,1,0:T(1,128)S(1)}, u32[]{:S(2)}, u32[]{:S(2)}) async-start(s32[16,1,16]{2,1,0:T(1,128)} %bitcast.4), calls=%async_computation | async-start | bytes 16384 | tf_op jit(solution)/shard_map/all_to_all | solution.py:110
  11.5 6.4 %copy.292 = bf16[1,8192,256]{1,2,0:T(8,128)(2,1)} copy(bf16[1,8192,256]{2,1,0:T(8,128)(2,1)} %param.7) | data formatting | bytes 8388608 | tf_op args[0]
  17.9 7.0 %fusion = f32[512,2,2,64]{0,3,2,1:T(8,128)S(1)} fusion(bf16[2,2,64,8192]{3,2,1,0:T(8,128)(2,1)} %bitcast.587, bf16[1,2,8192,512]{3,2,1,0:T(8,128)(2,1)} %param.8), kind=kOutput, calls=%fused_computation | convolution fusion | flops 2147483648 | bytes 13107200 | tf_op jit(solution)/shard_map/dot_general | solution.py:64
  25.0 3.6 %copy-done.3 = bf16[1,2,8192,512]{3,2,1,0:T(8,128)(2,1)S(1)} copy-done((bf16[1,2,8192,512]{3,2,1,0:T(8,128)(2,1)S(1)}, bf16[1,2,8192,512]{3,2,1,0:T(8,128)(2,1)}, u32[]{:S(2)}) %copy-start.3) | copy-done | bytes 16777240
  28.6 2.3 %fusion.2 = f32[512,2,2,64]{0,3,2,1:T(8,128)S(1)} fusion(bf16[2,2,64,8192]{3,2,1,0:T(8,128)(2,1)S(1)} %bitcast.588, bf16[1,2,8192,512]{3,2,1,0:T(8,128)(2,1)S(1)} %copy-done.3), kind=kOutput, calls=%fused_computation.2 | convolution fusion | flops 2147483648 | bytes 13107200 | tf_op jit(solution)/shard_map/dot_general | solution.py:61
  33.1 0.7 constant_dynamic-update-slice_fusion.124
  35.2 0.7 constant_dynamic-update-slice_fusion.121
  39.4 0.7 constant_dynamic-update-slice_fusion.115
  40.2 0.7 constant_dynamic-update-slice_fusion.114
  45.1 0.7 constant_dynamic-update-slice_fusion.107
  47.2 0.7 constant_dynamic-update-slice_fusion.104
  48.6 0.7 constant_dynamic-update-slice_fusion.102
  49.4 0.7 constant_dynamic-update-slice_fusion.101
  50.8 0.7 constant_dynamic-update-slice_fusion.99
  51.5 0.7 constant_dynamic-update-slice_fusion.98
  54.2 0.7 constant_dynamic-update-slice_fusion.94
  55.6 0.7 constant_dynamic-update-slice_fusion.92
  59.9 0.7 constant_dynamic-update-slice_fusion.86
  62.0 0.7 constant_dynamic-update-slice_fusion.83
  63.4 0.7 constant_dynamic-update-slice_fusion.81
  66.3 0.7 constant_dynamic-update-slice_fusion.77
  70.5 0.7 constant_dynamic-update-slice_fusion.71
  73.3 0.7 constant_dynamic-update-slice_fusion.67
  74.7 0.7 constant_dynamic-update-slice_fusion.65
  86.0 0.7 constant_dynamic-update-slice_fusion.49
  88.8 0.7 constant_dynamic-update-slice_fusion.45
  90.9 0.7 constant_dynamic-update-slice_fusion.42
  91.6 0.7 constant_dynamic-update-slice_fusion.41
  103.6 0.7 constant_dynamic-update-slice_fusion.24
  107.8 0.7 constant_dynamic-update-slice_fusion.18
  117.0 0.7 constant_dynamic-update-slice_fusion.5
  119.1 0.7 constant_dynamic-update-slice_fusion.2
  119.8 0.7 constant_dynamic-update-slice_fusion.1
  120.8 0.7 constant_dynamic-update-slice_fusion
  121.6 7.2 %all-to-all-start.2 = ((s32[16,1,16]{2,1,0:T(1,128)}), s32[16,1,16]{2,1,0:T(1,128)S(1)}, u32[]{:S(2)}, u32[]{:S(2)}) async-start(s32[16,1,16]{2,1,0:T(1,128)} %bitcast.7), calls=%async_computation.2 | async-start | bytes 16384 | tf_op jit(solution)/shard_map/all_to_all | solution.py:111
  128.8 7.0 %copy.293 = bf16[128,1,4,2,128]{4,2,3,1,0:T(4,128)(2,1)} copy(bf16[128,1,4,2,128]{2,4,3,1,0:T(8,128)(2,1)} %constant_dynamic-update-slice_fusion) | data formatting | bytes 524288 | tf_op jit(solution)/shard_map/stack | solution.py:77
  136.4 7.2 %all-to-all-start.1 = ((f32[16,16,2]{1,2,0:T(2,128)}), f32[16,16,2]{1,2,0:T(2,128)S(1)}, u32[]{:S(2)}, u32[]{:S(2)}) async-start(f32[16,16,2]{1,2,0:T(2,128)} %copy.287), calls=%async_computation.1 | async-start | bytes 32768 | tf_op jit(solution)/shard_map/all_to_all | solution.py:112
  144.0 7.3 %all-to-all-done.1 = f32[16,16,2]{1,2,0:T(2,128)S(1)} async-done(((f32[16,16,2]{1,2,0:T(2,128)}), f32[16,16,2]{1,2,0:T(2,128)S(1)}, u32[]{:S(2)}, u32[]{:S(2)}) %all-to-all-start.1) | async-done | bytes 2080 | tf_op jit(solution)/shard_map/all_to_all | solution.py:112
  151.3 6.4 %all-to-all-start.3 = ((bf16[128,1,4,2,128]{4,2,3,1,0:T(4,128)(2,1)}), bf16[128,1,4,2,128]{4,2,3,1,0:T(4,128)(2,1)S(1)}, u32[]{:S(2)}, u32[]{:S(2)}) async-start(bf16[128,1,4,2,128]{4,2,3,1,0:T(4,128)(2,1)} %copy.293), calls=%async_computation.3 | async-start | bytes 524288 | tf_op jit(solution)/shard_map/all_to_all | solution.py:76
  158.2 1.3 select_reduce_fusion
  159.4 8.9 %all-to-all-done.3 = bf16[128,1,4,2,128]{4,2,3,1,0:T(4,128)(2,1)S(1)} async-done(((bf16[128,1,4,2,128]{4,2,3,1,0:T(4,128)(2,1)}), bf16[128,1,4,2,128]{4,2,3,1,0:T(4,128)(2,1)S(1)}, u32[]{:S(2)}, u32[]{:S(2)}) %all-to-all-start.3) | async-done | bytes 262176 | tf_op jit(solution)/shard_map/all_to_all | solution.py:76
  168.6 2.7 %collective-permute-start = (bf16[4,128,128]{2,1,0:T(8,128)(2,1)S(1)}, bf16[4,128,128]{2,1,0:T(8,128)(2,1)S(1)}, u32[]{:S(2)}, u32[]{:S(2)}) collective-permute-start(bf16[4,128,128]{2,1,0:T(8,128)(2,1)S(1)} %fusion.8), channel_id=1, source_target_pairs={{0,8},{8,16},{16,24},{24,32},{32,40},{40,48},{48,56},{56,64},{64,7... | collective-permute-start | bytes 393224 | tf_op jit(solution)/shard_map/ppermute | solution.py:16
  171.3 1.3 collective-permute-start.1
  173.9 4.3 %collective-permute-done.1 = bf16[4,128,128]{2,1,0:T(8,128)(2,1)S(1)} collective-permute-done((bf16[4,128,128]{2,1,0:T(8,128)(2,1)S(1)}, bf16[4,128,128]{2,1,0:T(8,128)(2,1)S(1)}, u32[]{:S(2)}, u32[]{:S(2)}) %collective-permute-start.1) | collective-permute-done | bytes 131104 | tf_op jit(solution)/shard_map/ppermute | solution.py:17
  178.6 15.0 %all_to_all.27 = f32[16,16,128]{2,1,0:T(8,128)S(1)} all-to-all(f32[16,16,128]{2,1,0:T(8,128)S(1)} %fusion.387), channel_id=1, replica_groups=mesh['ma'=16,'band'=8] {'ma'}, dimensions={0} | all-to-all | bytes 262144 | tf_op jit(solution)/shard_map/all_to_all | solution.py:126
  193.6 0.9 fusion.19
  (141 shorter events, 75.2 us)
Async XLA Ops:
  2.9 125.9 %copy-start.1 = (f32[16,16,4]{1,0,2:T(8,128)}, f32[16,16,4]{1,0,2:T(8,128)S(1)}, u32[]{:S(2)}) copy-start(f32[16,16,4]{1,0,2:T(8,128)S(1)} %reshape.275) | copy-start | bytes 12292
  3.5 118.0 %all-to-all-start = ((s32[16,1,16]{2,1,0:T(1,128)}), s32[16,1,16]{2,1,0:T(1,128)S(1)}, u32[]{:S(2)}, u32[]{:S(2)}) async-start(s32[16,1,16]{2,1,0:T(1,128)} %bitcast.4), calls=%async_computation | async-start | bytes 16384 | tf_op jit(solution)/shard_map/all_to_all | solution.py:110
  17.9 7.1 %copy-start = (bf16[1,8192,256]{1,2,0:T(8,128)(2,1)S(1)}, bf16[1,8192,256]{1,2,0:T(8,128)(2,1)}, u32[]{:S(2)}) copy-start(bf16[1,8192,256]{1,2,0:T(8,128)(2,1)} %copy.292) | copy-start | bytes 12582916
  17.9 10.6 %copy-start.3 = (bf16[1,2,8192,512]{3,2,1,0:T(8,128)(2,1)S(1)}, bf16[1,2,8192,512]{3,2,1,0:T(8,128)(2,1)}, u32[]{:S(2)}) copy-start(bf16[1,2,8192,512]{3,2,1,0:T(8,128)(2,1)} %param.8) | copy-start | bytes 50331652
  84.6 36.0 %copy-start.2 = (s32[128]{0:T(128)S(1)}, s32[128]{0:T(128)}, u32[]{:S(2)}) copy-start(s32[128]{0:T(128)} %param.9) | copy-start | bytes 1540
  121.6 14.9 %all-to-all-start.2 = ((s32[16,1,16]{2,1,0:T(1,128)}), s32[16,1,16]{2,1,0:T(1,128)S(1)}, u32[]{:S(2)}, u32[]{:S(2)}) async-start(s32[16,1,16]{2,1,0:T(1,128)} %bitcast.7), calls=%async_computation.2 | async-start | bytes 16384 | tf_op jit(solution)/shard_map/all_to_all | solution.py:111
  128.8 7.0 %slice-start = ((f32[16,16,4]{1,0,2:T(8,128)}), f32[16,16,2]{1,0,2:T(8,128)S(1)}, s32[]{:S(2)}) async-start(f32[16,16,4]{1,0,2:T(8,128)} %copy-done.1), calls=%async_computation.5 | async-start | bytes 32768 | tf_op jit(solution)/shard_map/slice | solution.py:109
  136.4 14.8 %all-to-all-start.1 = ((f32[16,16,2]{1,2,0:T(2,128)}), f32[16,16,2]{1,2,0:T(2,128)S(1)}, u32[]{:S(2)}, u32[]{:S(2)}) async-start(f32[16,16,2]{1,2,0:T(2,128)} %copy.287), calls=%async_computation.1 | async-start | bytes 32768 | tf_op jit(solution)/shard_map/all_to_all | solution.py:112
  151.3 17.1 %all-to-all-start.3 = ((bf16[128,1,4,2,128]{4,2,3,1,0:T(4,128)(2,1)}), bf16[128,1,4,2,128]{4,2,3,1,0:T(4,128)(2,1)S(1)}, u32[]{:S(2)}, u32[]{:S(2)}) async-start(bf16[128,1,4,2,128]{4,2,3,1,0:T(4,128)(2,1)} %copy.293), calls=%async_computation.3 | async-start | bytes 524288 | tf_op jit(solution)/shard_map/all_to_all | solution.py:76
  168.6 5.3 %collective-permute-start = (bf16[4,128,128]{2,1,0:T(8,128)(2,1)S(1)}, bf16[4,128,128]{2,1,0:T(8,128)(2,1)S(1)}, u32[]{:S(2)}, u32[]{:S(2)}) collective-permute-start(bf16[4,128,128]{2,1,0:T(8,128)(2,1)S(1)} %fusion.8), channel_id=1, source_target_pairs={{0,8},{8,16},{16,24},{24,32},{32,40},{40,48},{48,56},{56,64},{64,7... | collective-permute-start | bytes 393224 | tf_op jit(solution)/shard_map/ppermute | solution.py:16
  171.3 6.9 %collective-permute-start.1 = (bf16[4,128,128]{2,1,0:T(8,128)(2,1)S(1)}, bf16[4,128,128]{2,1,0:T(8,128)(2,1)S(1)}, u32[]{:S(2)}, u32[]{:S(2)}) collective-permute-start(bf16[4,128,128]{2,1,0:T(8,128)(2,1)S(1)} %fusion.8), channel_id=1, source_target_pairs={{8,0},{16,8},{24,16},{32,24},{40,32},{48,40},{56,48},{64,56},{72,6... | collective-permute-start | bytes 393224 | tf_op jit(solution)/shard_map/ppermute | solution.py:17
